TPU v7x, 32 devices: a whole 2x2x4 slice. The times are simulated.
32 devices in a mesh: seq: 8 (over y, x, core), head: 4 (over z).
Axes of the slice: x: 2, y: 2, z: 4, core: 2. Of those that a mesh axis runs over, the one named last changes fastest.
Arguments:
- tokens: bfloat16 [8192, 1024], P(('seq', 'head')), may hold values from -6 to 6
- qkv_weight: bfloat16 [1024, 3, 1024], P(None, None, 'head'), may hold values from -0.1875 to 0.1875
- out_weight: bfloat16 [1024, 1024], P('head'), may hold values from -0.1875 to 0.1875
- up_weight: bfloat16 [1024, 2, 2816], P(None, None, 'head'), may hold values from -0.1875 to 0.1875
- down_weight: bfloat16 [2816, 1024], P('head'), may hold values from -0.109375 to 0.109375
- vocab_weight: bfloat16 [1024, 16384], P(None, 'head'), may hold values from -0.1875 to 0.1875
- persistent: bfloat16 [2, 16, 1024], P(None, None, 'head'), may hold values from -120 to 120
- norm_gains: float32 [3, 1024], replicated, may hold values from 0.5 to 1.5
- write_rate: float32 [8192, 8], P('seq', 'head'), may hold values from 0.02 to 0.2
- forget: float32 [128, 8], P('seq', 'head'), may hold values from 0 to 1
- momentum: float32 [128, 8], P('seq', 'head'), may hold values from 0.2 to 0.9
- prompt_spans: int32 [4], replicated, may hold values from 1 to 64, as said below
Outputs:
- logit_max: float32 [8192], P('seq')
- state_rms: float32 [4, 8], P(None, 'head')
Inputs may be any that keep to these rules, and one draw needn't show every extreme that they name: Prompt p holds prompt_spans[p] consecutive spans of 64 tokens, the prompts packed in order from token 0; they sum to 128, and prompt 1 is the longest, with exactly 64 spans.
All inputs are finite; a program needn't handle non-finite values.
Results may differ from a plain program's by a relative error of at most 0.0047.
Values may be sent and summed in bfloat16 or wider, within the bound.
No kernel may reach another device: no remote copies, remote signals or barrier semaphores. Data moves between devices by JAX's collectives and lax.ppermute only.
A program may use at most 128 MiB of HBM per device.

v0:
```python
import jax
import jax.numpy as jnp
from jax import lax
from jax.sharding import PartitionSpec as P

D = 1024
HS = 128
NPER = 16
SEG = 1024
CH = 64
SEQS = 4


eps_norm = 1e-05
eps_unit = 1e-06
score_scale = 10.0
masked_score = -1e30


def passed_along(array, axis, by):
    size = lax.axis_size(axis)
    pairs = [(i, i + by) for i in range(size) if 0 <= i + by < size]
    return lax.ppermute(array, axis, pairs)


def carried_in(part, axis, combine, identity):
    place = lax.axis_index(axis)
    gathered = jax.tree.map(lambda a: lax.all_gather(a, axis), part)
    state = jax.tree.map(lambda a, e: jnp.zeros_like(a) + jnp.asarray(e, a.dtype), part, identity)

    def one(step, state):
        return combine(
            state, jax.tree.map(lambda a: lax.dynamic_index_in_dim(a, step, 0, False), gathered)
        )

    return lax.fori_loop(0, place, one, state)


def rms_scale(values, gain):
    return values * lax.rsqrt(jnp.mean(values * values, axis=-1, keepdims=True) + eps_norm) * gain


def unit_rows(values):
    widened = values.astype(jnp.float32)
    return (
        widened * lax.rsqrt(jnp.sum(widened * widened, axis=-1, keepdims=True) + eps_unit)
    ).astype(jnp.bfloat16)


def segment_starts(positions, prompt_spans):
    prompt_ends = jnp.cumsum(prompt_spans)
    first_tokens = (prompt_ends - prompt_spans) * CH
    reached = positions[:, None] >= first_tokens[None, :]
    prompt_first = jnp.max(jnp.where(reached, first_tokens[None, :], 0), axis=1)
    return prompt_first + (positions - prompt_first) // SEG * SEG


def compose(later, earlier):
    return jnp.stack(
        [
            later[..., 0] * earlier[..., 0],
            later[..., 0] * earlier[..., 1] + later[..., 1] * earlier[..., 2],
            later[..., 2] * earlier[..., 2],
        ],
        axis=-1,
    )


def apply_map(coeffs, memory, moment):
    moved_memory = coeffs[:, 0, None, None] * memory + coeffs[:, 1, None, None] * moment
    return (moved_memory, coeffs[:, 2, None, None] * moment)


def chain_combine(earlier, later):
    moved_memory, moved_moment = apply_map(later[0], earlier[1], earlier[2])
    return (compose(later[0], earlier[0]), moved_memory + later[1], moved_moment + later[2])


def to_owners(local_rows, project):
    return project(lax.all_gather(local_rows, "head", axis=0, tiled=True), jnp.int32(0))


def from_owners(term, share_rows):
    return lax.psum_scatter(
        term(jnp.int32(0), share_rows * lax.axis_size("head")),
        "head",
        scatter_dimension=0,
        tiled=True,
    )


def local(
    tokens,
    qkv_weight,
    out_weight,
    up_weight,
    down_weight,
    vocab_weight,
    persistent,
    norm_gains,
    write_rate,
    forget,
    momentum,
    prompt_spans,
):
    share_rows = tokens.shape[0]
    head_count = lax.axis_size("head")
    seq_count = lax.axis_size("seq")
    block_rows = share_rows * head_count
    heads_here = write_rate.shape[1]
    current_width = heads_here * HS
    seq_index = lax.axis_index("seq")
    head_index = lax.axis_index("head")
    qkv_matrix = qkv_weight.reshape(D, 3 * current_width)
    highest = lax.Precision.HIGHEST

    def token_project(piece, start):
        normed = rms_scale(piece.astype(jnp.float32), norm_gains[0]).astype(jnp.bfloat16)
        projected = jnp.dot(normed, qkv_matrix, preferred_element_type=jnp.float32).astype(
            jnp.bfloat16
        )
        return projected

    gathered = to_owners(tokens, token_project)
    projected = gathered
    query_unit = unit_rows(projected[:, :current_width].reshape(block_rows, heads_here, HS))
    key_unit = unit_rows(
        projected[:, current_width : 2 * current_width].reshape(block_rows, heads_here, HS)
    )
    value_rows = projected[:, 2 * current_width :].reshape(block_rows, heads_here, HS)
    reach = SEG // block_rows
    moved_keys, moved_values = passed_along((key_unit, value_rows), "seq", 1)
    earlier_keys = [moved_keys]
    earlier_values = [moved_values]
    all_keys = jnp.concatenate(earlier_keys + [key_unit], axis=0)
    all_values = jnp.concatenate(earlier_values + [value_rows], axis=0)
    first_row = seq_index * block_rows
    query_positions = first_row + jnp.arange(block_rows, dtype=jnp.int32)
    key_positions = (
        first_row - reach * block_rows + jnp.arange((reach + 1) * block_rows, dtype=jnp.int32)
    )
    query_segments = segment_starts(query_positions, prompt_spans)
    key_segments = segment_starts(key_positions, prompt_spans)
    allowed = (
        (key_segments[None, :] == query_segments[:, None])
        & (key_positions[None, :] <= query_positions[:, None])
        & (key_positions[None, :] >= 0)
    )
    persist_keys = persistent[0].reshape(NPER, heads_here, HS)
    persist_values = persistent[1].reshape(NPER, heads_here, HS)
    scores = score_scale * jnp.einsum(
        "qhd,khd->hqk", query_unit, all_keys, preferred_element_type=jnp.float32
    )
    scores = jnp.where(allowed[None], scores, masked_score)
    extra = score_scale * jnp.einsum(
        "qhd,phd->hqp", query_unit, persist_keys, preferred_element_type=jnp.float32
    )
    top = jnp.maximum(jnp.max(scores, axis=-1), jnp.max(extra, axis=-1))[..., None]
    near = jnp.where(allowed[None], jnp.exp(scores - top), 0.0)
    far = jnp.exp(extra - top)
    total = jnp.sum(near, axis=-1, keepdims=True) + jnp.sum(far, axis=-1, keepdims=True)
    near_weights = (near / total).astype(jnp.bfloat16)
    far_weights = (far / total).astype(jnp.bfloat16)
    attended = jnp.einsum(
        "hqk,khd->qhd", near_weights, all_values, preferred_element_type=jnp.float32
    )
    attended = attended + jnp.einsum(
        "hqp,phd->qhd", far_weights, persist_values, preferred_element_type=jnp.float32
    )
    total_spans = block_rows // CH
    span_queries = query_unit.reshape(total_spans, CH, heads_here, HS)
    span_keys = key_unit.reshape(total_spans, CH, heads_here, HS)
    span_values = value_rows.reshape(total_spans, CH, heads_here, HS)
    span_rates = write_rate.reshape(total_spans, CH, heads_here)
    prompt_ends = jnp.cumsum(prompt_spans)
    first_spans = prompt_ends - prompt_spans
    span_ids = seq_index * total_spans + jnp.arange(total_spans, dtype=jnp.int32)
    keep = jnp.where(jnp.any(span_ids[:, None] == first_spans[None, :], axis=1), 0.0, 1.0).astype(
        jnp.float32
    )
    causal = (jnp.arange(CH)[:, None] >= jnp.arange(CH)[None, :]).astype(jnp.float32)
    values_wide = span_values.astype(jnp.float32)
    written = jnp.einsum(
        "cthi,cthj->chij",
        span_rates[..., None] * values_wide,
        span_keys.astype(jnp.float32),
        precision=highest,
    )
    affinity = jnp.einsum(
        "cthd,cshd->chts", span_queries, span_keys, preferred_element_type=jnp.float32
    )
    affinity = affinity * causal[None, None] * jnp.transpose(span_rates, (0, 2, 1))[:, :, None, :]
    local_recall = jnp.einsum("chts,cshi->cthi", affinity, values_wide, precision=highest)
    decay_memory = forget * keep[:, None]
    decay_moment = momentum * keep[:, None]
    identity_coeffs = jnp.tile(jnp.array([1.0, 0.0, 1.0], jnp.float32), (heads_here, 1))
    zero_state = jnp.zeros((heads_here, HS, HS), jnp.float32)

    def advance(carry, inputs):
        coeffs, memory, moment = carry
        current_written, memory_rate, moment_rate = inputs
        step_coeffs = jnp.stack([memory_rate, moment_rate, moment_rate], axis=-1)
        next_moment = moment_rate[:, None, None] * moment + current_written
        next_memory = (
            memory_rate[:, None, None] * memory
            + moment_rate[:, None, None] * moment
            + current_written
        )
        return ((compose(step_coeffs, coeffs), next_memory, next_moment), (coeffs, memory))

    (last_coeffs, last_memory, last_moment), (coeffs_before, memory_before) = lax.scan(
        advance, (identity_coeffs, zero_state, zero_state), (written, decay_memory, decay_moment)
    )
    _, incoming_memory, incoming_moment = carried_in(
        (last_coeffs, last_memory, last_moment),
        "seq",
        chain_combine,
        (identity_coeffs, zero_state, zero_state),
    )
    true_before = (
        memory_before
        + coeffs_before[..., 0, None, None] * incoming_memory[None]
        + coeffs_before[..., 1, None, None] * incoming_moment[None]
    )
    recalled = local_recall + jnp.einsum(
        "chij,cthj->cthi",
        true_before * keep[:, None, None, None],
        span_queries.astype(jnp.float32),
        precision=highest,
    )
    memory_after = jnp.concatenate([memory_before[1:], last_memory[None]], axis=0)
    coeffs_after = jnp.concatenate([coeffs_before[1:], last_coeffs[None]], axis=0)
    true_after = (
        memory_after
        + coeffs_after[..., 0, None, None] * incoming_memory[None]
        + coeffs_after[..., 1, None, None] * incoming_moment[None]
    )
    spread = jnp.sqrt(jnp.mean(true_after * true_after, axis=(2, 3)))
    hit_spans = span_ids[None, :] == (prompt_ends - 1)[:, None]
    state_slots = jnp.sum(jnp.where(hit_spans[:, :, None], spread[None], 0.0), axis=1)
    mixed = (
        (attended + recalled.reshape(block_rows, heads_here, HS))
        .astype(jnp.bfloat16)
        .reshape(block_rows, current_width)
    )
    ff_here = down_weight.shape[0]
    gate_up = up_weight.reshape(D, 2 * ff_here)

    def ffn_hidden(normed_rows):
        gated = jnp.dot(normed_rows, gate_up, preferred_element_type=jnp.float32)
        return (jax.nn.silu(gated[:, :ff_here]) * gated[:, ff_here:]).astype(jnp.bfloat16)

    def ffn_project(piece, start):
        return ffn_hidden(piece)

    def attn_term(start, count):
        return jnp.dot(mixed, out_weight, preferred_element_type=jnp.float32)

    residual = tokens.astype(jnp.float32) + from_owners(attn_term, share_rows)
    hidden = to_owners(rms_scale(residual, norm_gains[1]).astype(jnp.bfloat16), ffn_project)

    def down_term(start, count):
        return jnp.dot(hidden, down_weight, preferred_element_type=jnp.float32)

    second = residual + from_owners(down_term, share_rows)
    final = rms_scale(second, norm_gains[2]).astype(jnp.bfloat16)

    def vocab_maxima(piece, start):
        return jnp.max(jnp.dot(piece, vocab_weight, preferred_element_type=jnp.float32), axis=1)

    row_maxima = to_owners(final, vocab_maxima)
    token_total = block_rows * seq_count
    logit_full = lax.dynamic_update_slice(
        jnp.full((token_total,), masked_score, jnp.float32), row_maxima, (first_row,)
    )
    norm_full = lax.dynamic_update_slice(
        jnp.zeros((SEQS, heads_here * head_count), jnp.float32),
        state_slots,
        (0, head_index * heads_here),
    )
    logit_full, norm_full = lax.pmax((logit_full, norm_full), ("seq", "head"))
    logit_max = lax.dynamic_slice(logit_full, (first_row,), (block_rows,))
    state_rms = lax.dynamic_slice(norm_full, (0, head_index * heads_here), (SEQS, heads_here))
    return (logit_max, state_rms)


def solution(mesh):
    in_specs = (
        P(("seq", "head"), None),
        P(None, None, "head"),
        P("head", None),
        P(None, None, "head"),
        P("head", None),
        P(None, "head"),
        P(None, None, "head"),
        P(),
        P("seq", "head"),
        P("seq", "head"),
        P("seq", "head"),
        P(),
    )
    out_specs = (P("seq"), P(None, "head"))
    return jax.shard_map(local, mesh=mesh, in_specs=in_specs, out_specs=out_specs, check_vma=False)
```

profile of v0, /device:TPU:0, one launch (start us, length us, event | category | flops | bytes accessed | tf_op | source)
XLA Modules:
  0.0 530.7 jit_solution(4990581086919574727)
XLA Ops:
  16.5 41.8 %all-gather.10.cloned.1.call-done = bf16[1024,1024]{1,0:T(8,128)(2,1)} async-done(((bf16[256,1024]{1,0:T(8,128)(2,1)}), bf16[1024,1024]{1,0:T(8,128)(2,1)}) %all-gather.10.cloned.1.call-update) | async-done | bytes 2097168 | tf_op jit(solution)/shard_map/all_gather | solution.py:80
  60.5 3.3 fusion.23
  72.7 3.5 copy.206
  76.2 3.1 convert_multiply_fusion.2
  79.2 3.5 fusion.44
  82.8 29.3 %while.34 = (s32[]{:T(128)}, f32[2,3]{0,1:T(4,128)S(1)}, f32[2,128,128]{2,1,0:T(8,128)S(1)}, f32[2,128,128]{2,1,0:T(8,128)S(1)}, f32[16,2,3]{2,1,0:T(2,128)S(1)}...) while((s32[]{:T(128)}, f32[2,3]{0,1:T(4,128)S(1)}, ...), condition=%wide.region_12.13_spmd.clone, body=%wide.region_11.12_spmd.clone.sunk | while | flops 262167 | bytes 919908 | solution.py:211
  114.2 6.5 %and_and_fusion = pred[1024,2048]{1,0:T(8,128)(4,1)} fusion(s32[2048]{0:T(1024)S(1)} %iota_add_fusion, s32[2048]{0:T(1024)S(1)} %fusion.59, s32[1024]{0:T(1024)S(1)} %iota_add_fusion.1, s32[1024]{0:T(1024)S(1)} %fusion.66, pred[2048]{0:T(1024)(128)(4,1)S(1)} %fusion.63), kind=kLoop, calls=%fused_computation.25 | loop fusion | flops 8388608 | bytes 2123776 | tf_op jit(solution)/shard_map/and | solution.py:145
  129.8 3.7 collective-permute-start.1
  133.6 9.2 %all-gather.3 = f32[8,2,3]{2,1,0:T(2,128)} all-gather(f32[1,2,3]{2,1,0:T(2,128)S(1)} %bitcast.116), channel_id=2, replica_groups=mesh['seq'=8,'head'=4] {'seq'}, dimensions={0}, use_global_device_ids=true | all-gather | bytes 216 | tf_op jit(solution)/shard_map/all_gather | solution.py:28
  145.8 3.5 copy.203
  152.9 3.3 fusion.32
  156.2 4.9 fusion.3
  161.2 5.6 %fusion.4 = f32[2,1024]{1,0:T(2,128)S(1)} fusion(f32[2,1024,2048]{2,1,0:T(8,128)S(1)} %get-tuple-element.215, f32[2,1024]{1,0:T(2,128)S(1)} %max.11, pred[1024,2048]{1,0:T(8,128)(4,1)S(1)} %copy-done.10), kind=kLoop, calls=%fused_computation.24 | loop fusion | flops 20969472 | bytes 18890752 | tf_op jit(solution)/shard_map/reduce_sum | solution.py:161
  168.2 4.5 all-gather.16.cloned.1.call-done
  173.5 4.3 fusion.29
  182.1 10.5 %fusion.36 = bf16[1024,2,128]{0,2,1:T(8,128)(2,1)S(1)} fusion(f32[1024,2,128]{0,2,1:T(8,128)} %copy.219, f32[1024,2,128]{0,2,1:T(8,128)} %convolution_bitcast_fusion, f32[2,1024,2048]{2,1,0:T(8,128)} %copy-done.5, f32[2,1024]{1,0:T(2,128)S(1)} %add.226, f32[2,1024]{1,0:T(2,128)S(1)} %max.11, pred[1024,2048]{1,0:T(8,128)(4,1)} %and_and_fusion, ...), kind=kOutput, calls=%fused_computation.59 | convolution fusion | flops 1101791232 | bytes 22560768 | tf_op jit(solution)/shard_map/hqk,khd->qhd/dot_general | solution.py:164
  195.4 90.1 %reduce-scatter.3.cloned.1.call-done = f32[256,1024]{1,0:T(8,128)} async-done(((f32[1024,1024]{1,0:T(8,128)}), f32[256,1024]{1,0:T(8,128)}) %reduce-scatter.3.cloned.1.call-update) | async-done | bytes 1048592 | tf_op jit(solution)/shard_map/reduce_scatter | solution.py:84
  288.2 46.6 %all-gather.12.cloned.1.call-done = bf16[1024,1024]{1,0:T(8,128)(2,1)} async-done(((bf16[256,1024]{1,0:T(8,128)(2,1)}), bf16[1024,1024]{1,0:T(8,128)(2,1)}) %all-gather.12.cloned.1.call-update) | async-done | bytes 2097168 | tf_op jit(solution)/shard_map/all_gather | solution.py:80
  334.7 5.2 fusion.80
  339.9 3.8 fusion.26
  344.0 75.3 %reduce-scatter.5.cloned.1.call-done = f32[256,1024]{1,0:T(8,128)} async-done(((f32[1024,1024]{1,0:T(8,128)}), f32[256,1024]{1,0:T(8,128)}) %reduce-scatter.5.cloned.1.call-update) | async-done | bytes 1048592 | tf_op jit(solution)/shard_map/reduce_scatter | solution.py:84
  430.6 39.5 %all-gather.14.cloned.1.call-done = bf16[1024,1024]{1,0:T(8,128)(2,1)} async-done(((bf16[256,1024]{1,0:T(8,128)(2,1)}), bf16[1024,1024]{1,0:T(8,128)(2,1)}) %all-gather.14.cloned.1.call-update) | async-done | bytes 2097168 | tf_op jit(solution)/shard_map/all_gather | solution.py:80
  470.1 12.9 %convolution_reduce_fusion = f32[1024]{0:T(1024)S(1)} fusion(bf16[1024,1024]{1,0:T(8,128)(2,1)} %all-gather.14.cloned.1.call-done, bf16[1024,4096]{1,0:T(8,128)(2,1)} %param.22), kind=kOutput, calls=%fused_computation.32 | convolution fusion | flops 8594127872 | bytes 10489856 | tf_op jit(solution)/shard_map/dot_general | solution.py:269
  483.3 39.0 %all-reduce = (f32[8192]{0:T(1024)S(1)}, f32[4,8]{0,1:T(8,128)S(1)}) all-reduce(f32[8192]{0:T(1024)S(1)} %dynamic_update_slice.14, f32[4,8]{0,1:T(8,128)S(1)} %constant_dynamic-update-slice_fusion.1), channel_id=1, replica_groups=mesh['seq'=8,'head'=4] {'seq','head'}, use_global_device_ids=true, to_apply=%region_20.21 | all-reduce | flops 8224 | bytes 65792 | tf_op jit(solution)/shard_map/pmax | solution.py:281
  (284 shorter events, 91.5 us)
Async XLA Ops:
  7.2 327.6 %copy-start = (bf16[1024,2,704]{0,2,1:T(8,128)(2,1)S(1)}, bf16[1024,2,704]{0,2,1:T(8,128)(2,1)}, u32[]{:S(2)}) copy-start(bf16[1024,2,704]{0,2,1:T(8,128)(2,1)} %param.20) | copy-start | bytes 8650756
  7.2 7.7 %copy-start.29 = (s32[4]{0:T(128)S(1)}, s32[4]{0:T(128)}, u32[]{:S(2)}) copy-start(s32[4]{0:T(128)} %param.28) | copy-start | bytes 52
  7.2 8.6 %copy-start.24 = (bf16[2,16,256]{2,1,0:T(8,128)(2,1)S(1)}, bf16[2,16,256]{2,1,0:T(8,128)(2,1)}, u32[]{:S(2)}) copy-start(bf16[2,16,256]{2,1,0:T(8,128)(2,1)} %param.23) | copy-start | bytes 49156
  7.2 8.6 %copy-start.25 = (f32[3,1024]{1,0:T(4,128)S(1)}, f32[3,1024]{1,0:T(4,128)}, u32[]{:S(2)}) copy-start(f32[3,1024]{1,0:T(4,128)} %param.24) | copy-start | bytes 36868
  7.2 51.1 %all-gather.10.cloned.1.call-start = ((), (), s32[]{:S(2)}) async-start(), calls=%async_computation.2 | async-start | bytes 2621440 | tf_op jit(solution)/shard_map/all_gather | solution.py:80
  7.9 160.3 %all-gather.18.cloned.1.call-start = ((), (), s32[]{:S(2)}) async-start(), calls=%async_computation.8 | async-start | bytes 1179648 | tf_op jit(solution)/shard_map/all_gather | solution.py:28
  112.2 13.5 %copy-start.1 = (f32[2,128,128]{2,1,0:T(8,128)}, f32[2,128,128]{2,1,0:T(8,128)S(1)}, u32[]{:S(2)}) copy-start(f32[2,128,128]{2,1,0:T(8,128)S(1)} %get-tuple-element.115) | copy-start | bytes 393220
  112.2 37.1 %copy-start.18 = (f32[16,2,3]{2,1,0:T(2,128)}, f32[16,2,3]{2,1,0:T(2,128)S(1)}, u32[]{:S(2)}) copy-start(f32[16,2,3]{2,1,0:T(2,128)S(1)} %get-tuple-element.113) | copy-start | bytes 1156
  112.8 59.9 %all-gather.16.cloned.1.call-start = ((), (), s32[]{:S(2)}) async-start(), calls=%async_computation.7 | async-start | bytes 1179648 | tf_op jit(solution)/shard_map/all_gather | solution.py:28
  120.6 61.5 %collective-permute-start = (bf16[1024,2,128]{0,2,1:T(8,128)(2,1)}, bf16[1024,2,128]{0,2,1:T(8,128)(2,1)}, u32[]{:S(2)}, u32[]{:S(2)}) collective-permute-start(bf16[1024,2,128]{0,2,1:T(8,128)(2,1)} %bitcast.5), channel_id=1, source_target_pairs={{0,4},{4,8},{8,12},{12,16},{16,20},{20,24},{24,28},{1,5},{5,9},{9,... | collective-permute-start | bytes 1572872 | tf_op jit(solution)/shard_map/ppermute | solution.py:23
  129.8 26.4 %collective-permute-start.1 = (bf16[1024,2,128]{2,0,1:T(8,128)(2,1)S(1)}, bf16[1024,2,128]{2,0,1:T(8,128)(2,1)}, u32[]{:S(2)}, u32[]{:S(2)}) collective-permute-start(bf16[1024,2,128]{2,0,1:T(8,128)(2,1)S(1)} %multiply_convert_fusion.4), channel_id=1, source_target_pairs={{0,4},{4,8},{8,12},{12,16},{16,20},{20,24},{24,28},{1,5},{5,9},{9,... | collective-permute-start | bytes 1572872 | tf_op jit(solution)/shard_map/ppermute | solution.py:23
  133.6 12.1 %copy-start.26 = (f32[2,3]{1,0:T(2,128)}, f32[2,3]{1,0:T(2,128)S(1)}, u32[]{:S(2)}) copy-start(f32[2,3]{1,0:T(2,128)S(1)} %copy.215) | copy-start | bytes 76
  151.0 134.6 %reduce-scatter.3.cloned.1.call-start = ((), (), s32[]{:S(2)}) async-start(), calls=%async_computation.3 | async-start | bytes 5242880 | tf_op jit(solution)/shard_map/reduce_scatter | solution.py:84
  151.0 5.2 copy-start.10
  151.0 5.2 copy-start.15
  161.1 5.7 %copy-start.5 = (f32[2,1024,2048]{2,1,0:T(8,128)}, f32[2,1024,2048]{2,1,0:T(8,128)S(1)}, u32[]{:S(2)}) copy-start(f32[2,1024,2048]{2,1,0:T(8,128)S(1)} %get-tuple-element.215) | copy-start | bytes 50331652
  161.2 5.7 %copy-start.22 = (bf16[16,2,128]{2,1,0:T(2,128)(2,1)S(1)}, bf16[16,2,128]{2,1,0:T(2,128)(2,1)}, u32[]{:S(2)}) copy-start(bf16[16,2,128]{2,1,0:T(2,128)(2,1)} %reshape_squeeze.7) | copy-start | bytes 24580
  182.1 10.5 %copy-start.17 = (bf16[256,1024]{1,0:T(8,128)(2,1)S(1)}, bf16[256,1024]{1,0:T(8,128)(2,1)}, u32[]{:S(2)}) copy-start(bf16[256,1024]{1,0:T(8,128)(2,1)} %param.19) | copy-start | bytes 1572868
  195.3 90.2 %copy-start.6 = (bf16[256,1024]{1,0:T(8,128)(2,1)S(1)}, bf16[256,1024]{1,0:T(8,128)(2,1)}, u32[]{:S(2)}) copy-start(bf16[256,1024]{1,0:T(8,128)(2,1)} %param.17) | copy-start | bytes 1572868
  195.3 91.8 %copy-start.23 = (f32[1,1024]{1,0:T(1,128)S(1)}, f32[1,1024]{1,0:T(1,128)}, u32[]{:S(2)}) copy-start(f32[1,1024]{1,0:T(1,128)} %get-tuple-element.208) | copy-start | bytes 12292
  195.3 139.4 %all-gather.12.cloned.1.call-start = ((), (), s32[]{:S(2)}) async-start(), calls=%async_computation.4 | async-start | bytes 2621440 | tf_op jit(solution)/shard_map/all_gather | solution.py:80
  288.1 131.3 %reduce-scatter.5.cloned.1.call-start = ((), (), s32[]{:S(2)}) async-start(), calls=%async_computation.5 | async-start | bytes 5242880 | tf_op jit(solution)/shard_map/reduce_scatter | solution.py:84
  334.7 5.2 copy-start.31
  343.7 126.3 %all-gather.14.cloned.1.call-start = ((), (), s32[]{:S(2)}) async-start(), calls=%async_computation.6 | async-start | bytes 2621440 | tf_op jit(solution)/shard_map/all_gather | solution.py:80
  (18 other events, 45.6 us)
Sparse Core Ops, SparseCore 0:
  9.6 48.6 all-gather.9
  113.0 23.5 all-gather.17
  151.1 21.6 all-gather.15
  195.5 90.0 reduce-scatter.2
  288.2 46.4 all-gather.11
  343.9 75.4 reduce-scatter.4
  423.4 46.6 all-gather.13
where the time goes:
time: 540 us; the launch traced here: 531 us
  waiting for transfers between devices  299 us (55%)
  other arithmetic  58.8 us (11%)
  matrix products  58.3 us (11%)
  blocking collectives  48.2 us (9%)
  local copies, waits for them, and re-layouts  44.2 us (8%)
  between operations  15.1 us (3%)
  starting transfers between devices  6.75 us (1%)
    reduce_scatter x2, waiting for transfers between devices, from_owners(): lax.psum_scatter(term(jnp.int32(0), share_rows * lax.axis_size('head')),...  165 us
    all_gather x3, waiting for transfers between devices, to_owners(): lax.all_gather(local_rows, 'head', axis=0, tiled=True)  128 us
    pmax x1, blocking collectives, local(): logit_full, norm_full = lax.pmax((logit_full, norm_full), ('seq', 'head'))  39 us
    convert_element_type x6, local copies, waits for them, and re-layouts, unit_rows(): widened = values.astype(jnp.float32)  17.8 us
    add x16, other arithmetic, advance(): next_moment = moment_rate[:, None, None] * moment + current_written  16 us
    dot_general x1, matrix products, vocab_maxima(): jnp.dot(piece, vocab_weight, preferred_element_type=jnp.float32)  12.9 us
  transfers between devices with their start and end apart: 9, of which 6 were waited for; matrix products, arithmetic and copies ran while one was open for 12% of the time, Pallas kernels for 0%

commit v1 on v0

--- a/solution.py
+++ b/solution.py
@@ -269,18 +269,8 @@
         return jnp.max(jnp.dot(piece, vocab_weight, preferred_element_type=jnp.float32), axis=1)
 
     row_maxima = to_owners(final, vocab_maxima)
-    token_total = block_rows * seq_count
-    logit_full = lax.dynamic_update_slice(
-        jnp.full((token_total,), masked_score, jnp.float32), row_maxima, (first_row,)
-    )
-    norm_full = lax.dynamic_update_slice(
-        jnp.zeros((SEQS, heads_here * head_count), jnp.float32),
-        state_slots,
-        (0, head_index * heads_here),
-    )
-    logit_full, norm_full = lax.pmax((logit_full, norm_full), ("seq", "head"))
-    logit_max = lax.dynamic_slice(logit_full, (first_row,), (block_rows,))
-    state_rms = lax.dynamic_slice(norm_full, (0, head_index * heads_here), (SEQS, heads_here))
+    logit_max = lax.pmax(row_maxima, "head")
+    state_rms = lax.psum(state_slots, "seq")
     return (logit_max, state_rms)
 
 

time: 540 us -> 509 us (0.943)
  waiting for transfers between devices: 299 us -> 284 us
  blocking collectives: 48.2 us -> 33.9 us
    pmax x1, blocking collectives: 39 us -> 9.87 us  [local(): logit_max = lax.pmax(row_maxima, 'head')]
    all_gather x3, waiting for transfers between devices: 128 us -> 113 us  [to_owners(): lax.all_gather(local_rows, 'head', axis=0, tiled=True)]
    psum x0 -> x1, blocking collectives: none -> 14.6 us  [local(): state_rms = lax.psum(state_slots, 'seq')]
  transfers between devices with their start and end apart: 9 -> 9, of which waited for: 6 -> 6; matrix products, arithmetic and copies ran while one was open for 12% -> 13% of each run, Pallas kernels for 0% -> 0%
where the time goes in v1:
time: 509 us; the launch traced here: 500 us
  waiting for transfers between devices  284 us (56%)
  other arithmetic  58.9 us (12%)
  matrix products  58.3 us (11%)
  local copies, waits for them, and re-layouts  42.7 us (8%)
  blocking collectives  33.9 us (7%)
  between operations  14.9 us (3%)
  starting transfers between devices  6.71 us (1%)
    reduce_scatter x2, waiting for transfers between devices, from_owners(): lax.psum_scatter(term(jnp.int32(0), share_rows * lax.axis_size('head')),...  166 us
    all_gather x3, waiting for transfers between devices, to_owners(): lax.all_gather(local_rows, 'head', axis=0, tiled=True)  113 us
    convert_element_type x6, local copies, waits for them, and re-layouts, unit_rows(): widened = values.astype(jnp.float32)  17.8 us
    add x16, other arithmetic, advance(): next_moment = moment_rate[:, None, None] * moment + current_written  16 us
    psum x1, blocking collectives, local(): state_rms = lax.psum(state_slots, 'seq')  14.6 us
    dot_general x1, matrix products, vocab_maxima(): jnp.dot(piece, vocab_weight, preferred_element_type=jnp.float32)  12.9 us
    dynamic_update_slice x16, other arithmetic, local(): lax.scan(advance, (identity_coeffs, zero_state, zero_state), (written, de...  10.7 us
    dot_general x1, matrix products, local(): jnp.einsum('hqk,khd->qhd', near_weights, all_values, preferred_element_ty...  10.5 us
  transfers between devices with their start and end apart: 9, of which 6 were waited for; matrix products, arithmetic and copies ran while one was open for 13% of the time, Pallas kernels for 0%

profile of v1, /device:TPU:0, one launch (start us, length us, event | category | flops | bytes accessed | tf_op | source)
XLA Modules:
  0.0 499.9 jit_solution(11633201319285851177)
XLA Ops:
  16.5 41.8 %all-gather.10.cloned.1.call-done = bf16[1024,1024]{1,0:T(8,128)(2,1)} async-done(((bf16[256,1024]{1,0:T(8,128)(2,1)}), bf16[1024,1024]{1,0:T(8,128)(2,1)}) %all-gather.10.cloned.1.call-update) | async-done | bytes 2097168 | tf_op jit(solution)/shard_map/all_gather | solution.py:80
  60.5 3.3 fusion.23
  72.7 3.5 copy.206
  79.2 3.5 fusion.44
  82.8 29.4 %while.34 = (s32[]{:T(128)}, f32[2,3]{0,1:T(4,128)S(1)}, f32[2,128,128]{2,1,0:T(8,128)S(1)}, f32[2,128,128]{2,1,0:T(8,128)S(1)}, f32[16,2,3]{2,1,0:T(2,128)S(1)}...) while((s32[]{:T(128)}, f32[2,3]{0,1:T(4,128)S(1)}, ...), condition=%wide.region_12.13_spmd.clone, body=%wide.region_11.12_spmd.clone.sunk | while | flops 262167 | bytes 919908 | solution.py:211
  114.2 6.4 %and_and_fusion = pred[1024,2048]{1,0:T(8,128)(4,1)} fusion(s32[2048]{0:T(1024)S(1)} %iota_add_fusion, s32[2048]{0:T(1024)S(1)} %fusion.59, s32[1024]{0:T(1024)S(1)} %iota_add_fusion.1, s32[1024]{0:T(1024)S(1)} %fusion.66, pred[2048]{0:T(1024)(128)(4,1)S(1)} %fusion.63), kind=kLoop, calls=%fused_computation.25 | loop fusion | flops 8388608 | bytes 2123776 | tf_op jit(solution)/shard_map/and | solution.py:145
  129.8 3.7 collective-permute-start.1
  133.6 9.4 %all-gather.3 = f32[8,2,3]{2,1,0:T(2,128)} all-gather(f32[1,2,3]{2,1,0:T(2,128)S(1)} %bitcast.116), channel_id=2, replica_groups=mesh['seq'=8,'head'=4] {'seq'}, dimensions={0}, use_global_device_ids=true | all-gather | bytes 216 | tf_op jit(solution)/shard_map/all_gather | solution.py:28
  145.9 3.5 copy.203
  153.0 3.3 fusion.32
  156.3 4.9 fusion.3
  161.4 5.6 %fusion.4 = f32[2,1024]{1,0:T(2,128)S(1)} fusion(f32[2,1024,2048]{2,1,0:T(8,128)S(1)} %get-tuple-element.213, f32[2,1024]{1,0:T(2,128)S(1)} %max.9, pred[1024,2048]{1,0:T(8,128)(4,1)S(1)} %copy-done.10), kind=kLoop, calls=%fused_computation.24 | loop fusion | flops 20969472 | bytes 18890752 | tf_op jit(solution)/shard_map/reduce_sum | solution.py:161
  168.4 4.3 all-gather.16.cloned.1.call-done
  173.4 4.3 fusion.29
  182.1 10.5 %fusion.36 = bf16[1024,2,128]{0,2,1:T(8,128)(2,1)S(1)} fusion(f32[1024,2,128]{0,2,1:T(8,128)} %copy.219, f32[1024,2,128]{0,2,1:T(8,128)} %convolution_bitcast_fusion, f32[2,1024,2048]{2,1,0:T(8,128)} %copy-done.5, f32[2,1024]{1,0:T(2,128)S(1)} %add.220, f32[2,1024]{1,0:T(2,128)S(1)} %max.9, pred[1024,2048]{1,0:T(8,128)(4,1)} %and_and_fusion, ...), kind=kOutput, calls=%fused_computation.59 | convolution fusion | flops 1101791232 | bytes 22560768 | tf_op jit(solution)/shard_map/hqk,khd->qhd/dot_general | solution.py:164
  195.4 90.2 %reduce-scatter.3.cloned.1.call-done = f32[256,1024]{1,0:T(8,128)} async-done(((f32[1024,1024]{1,0:T(8,128)}), f32[256,1024]{1,0:T(8,128)}) %reduce-scatter.3.cloned.1.call-update) | async-done | bytes 1048592 | tf_op jit(solution)/shard_map/reduce_scatter | solution.py:84
  288.2 46.5 %all-gather.12.cloned.1.call-done = bf16[1024,1024]{1,0:T(8,128)(2,1)} async-done(((bf16[256,1024]{1,0:T(8,128)(2,1)}), bf16[1024,1024]{1,0:T(8,128)(2,1)}) %all-gather.12.cloned.1.call-update) | async-done | bytes 2097168 | tf_op jit(solution)/shard_map/all_gather | solution.py:80
  334.7 5.2 %fusion.80 = f32[1024,1408]{1,0:T(8,128)S(1)} fusion(bf16[1024,1024]{1,0:T(8,128)(2,1)} %all-gather.12.cloned.1.call-done, bf16[1024,1408]{0,1:T(8,128)(2,1)S(1)} %bitcast.104), kind=kOutput, calls=%fused_computation.154 | convolution fusion | flops 2952790016 | bytes 10747904 | tf_op jit(solution)/shard_map/dot_general | solution.py:250
  339.9 3.8 fusion.26
  344.0 75.4 %reduce-scatter.5.cloned.1.call-done = f32[256,1024]{1,0:T(8,128)} async-done(((f32[1024,1024]{1,0:T(8,128)}), f32[256,1024]{1,0:T(8,128)}) %reduce-scatter.5.cloned.1.call-update) | async-done | bytes 1048592 | tf_op jit(solution)/shard_map/reduce_scatter | solution.py:84
  430.6 14.6 %psum.7 = f32[4,2]{0,1:T(2,128)} all-reduce(f32[4,2]{0,1:T(2,128)S(1)} %select_reduce_fusion.2), channel_id=1, replica_groups=mesh['seq'=8,'head'=4] {'seq'}, use_global_device_ids=true, to_apply=%region_23.24 | all-reduce | flops 8 | bytes 64 | tf_op jit(solution)/shard_map/psum | solution.py:273
  445.2 24.9 %all-gather.14.cloned.1.call-done = bf16[1024,1024]{1,0:T(8,128)(2,1)} async-done(((bf16[256,1024]{1,0:T(8,128)(2,1)}), bf16[1024,1024]{1,0:T(8,128)(2,1)}) %all-gather.14.cloned.1.call-update) | async-done | bytes 2097168 | tf_op jit(solution)/shard_map/all_gather | solution.py:80
  470.1 12.9 %convolution_reduce_fusion = f32[1024]{0:T(1024)S(1)} fusion(bf16[1024,1024]{1,0:T(8,128)(2,1)} %all-gather.14.cloned.1.call-done, bf16[1024,4096]{1,0:T(8,128)(2,1)} %param.22), kind=kOutput, calls=%fused_computation.32 | convolution fusion | flops 8594127872 | bytes 10489856 | tf_op jit(solution)/shard_map/dot_general | solution.py:269
  483.0 9.9 %pmax.7 = f32[1024]{0:T(1024)} all-reduce(f32[1024]{0:T(1024)S(1)} %convolution_reduce_fusion), channel_id=1, replica_groups=mesh['seq'=8,'head'=4] {'head'}, use_global_device_ids=true, to_apply=%region_20.21 | all-reduce | flops 1024 | bytes 8192 | tf_op jit(solution)/shard_map/pmax | solution.py:272
  (279 shorter events, 93.0 us)
Async XLA Ops:
  7.2 327.6 %copy-start = (bf16[1024,2,704]{0,2,1:T(8,128)(2,1)S(1)}, bf16[1024,2,704]{0,2,1:T(8,128)(2,1)}, u32[]{:S(2)}) copy-start(bf16[1024,2,704]{0,2,1:T(8,128)(2,1)} %param.20) | copy-start | bytes 8650756
  7.2 7.7 %copy-start.29 = (s32[4]{0:T(128)S(1)}, s32[4]{0:T(128)}, u32[]{:S(2)}) copy-start(s32[4]{0:T(128)} %param.28) | copy-start | bytes 52
  7.2 8.6 %copy-start.24 = (bf16[2,16,256]{2,1,0:T(8,128)(2,1)S(1)}, bf16[2,16,256]{2,1,0:T(8,128)(2,1)}, u32[]{:S(2)}) copy-start(bf16[2,16,256]{2,1,0:T(8,128)(2,1)} %param.23) | copy-start | bytes 49156
  7.2 8.6 %copy-start.25 = (f32[3,1024]{1,0:T(4,128)S(1)}, f32[3,1024]{1,0:T(4,128)}, u32[]{:S(2)}) copy-start(f32[3,1024]{1,0:T(4,128)} %param.24) | copy-start | bytes 36868
  7.2 51.1 %all-gather.10.cloned.1.call-start = ((), (), s32[]{:S(2)}) async-start(), calls=%async_computation.2 | async-start | bytes 2621440 | tf_op jit(solution)/shard_map/all_gather | solution.py:80
  7.9 160.4 %all-gather.18.cloned.1.call-start = ((), (), s32[]{:S(2)}) async-start(), calls=%async_computation.8 | async-start | bytes 1179648 | tf_op jit(solution)/shard_map/all_gather | solution.py:28
  112.2 13.5 %copy-start.1 = (f32[2,128,128]{2,1,0:T(8,128)}, f32[2,128,128]{2,1,0:T(8,128)S(1)}, u32[]{:S(2)}) copy-start(f32[2,128,128]{2,1,0:T(8,128)S(1)} %get-tuple-element.115) | copy-start | bytes 393220
  112.2 37.3 %copy-start.18 = (f32[16,2,3]{2,1,0:T(2,128)}, f32[16,2,3]{2,1,0:T(2,128)S(1)}, u32[]{:S(2)}) copy-start(f32[16,2,3]{2,1,0:T(2,128)S(1)} %get-tuple-element.113) | copy-start | bytes 1156
  112.8 59.9 %all-gather.16.cloned.1.call-start = ((), (), s32[]{:S(2)}) async-start(), calls=%async_computation.7 | async-start | bytes 1179648 | tf_op jit(solution)/shard_map/all_gather | solution.py:28
  120.6 61.5 %collective-permute-start = (bf16[1024,2,128]{0,2,1:T(8,128)(2,1)}, bf16[1024,2,128]{0,2,1:T(8,128)(2,1)}, u32[]{:S(2)}, u32[]{:S(2)}) collective-permute-start(bf16[1024,2,128]{0,2,1:T(8,128)(2,1)} %bitcast.5), channel_id=1, source_target_pairs={{0,4},{4,8},{8,12},{12,16},{16,20},{20,24},{24,28},{1,5},{5,9},{9,... | collective-permute-start | bytes 1572872 | tf_op jit(solution)/shard_map/ppermute | solution.py:23
  129.8 26.6 %collective-permute-start.1 = (bf16[1024,2,128]{2,0,1:T(8,128)(2,1)S(1)}, bf16[1024,2,128]{2,0,1:T(8,128)(2,1)}, u32[]{:S(2)}, u32[]{:S(2)}) collective-permute-start(bf16[1024,2,128]{2,0,1:T(8,128)(2,1)S(1)} %multiply_convert_fusion.4), channel_id=1, source_target_pairs={{0,4},{4,8},{8,12},{12,16},{16,20},{20,24},{24,28},{1,5},{5,9},{9,... | collective-permute-start | bytes 1572872 | tf_op jit(solution)/shard_map/ppermute | solution.py:23
  133.6 12.2 %copy-start.26 = (f32[2,3]{1,0:T(2,128)}, f32[2,3]{1,0:T(2,128)S(1)}, u32[]{:S(2)}) copy-start(f32[2,3]{1,0:T(2,128)S(1)} %copy.215) | copy-start | bytes 76
  151.1 134.4 %reduce-scatter.3.cloned.1.call-start = ((), (), s32[]{:S(2)}) async-start(), calls=%async_computation.3 | async-start | bytes 5242880 | tf_op jit(solution)/shard_map/reduce_scatter | solution.py:84
  151.2 5.2 %copy-start.10 = (pred[1024,2048]{1,0:T(8,128)(4,1)S(1)}, pred[1024,2048]{1,0:T(8,128)(4,1)}, u32[]{:S(2)}) copy-start(pred[1024,2048]{1,0:T(8,128)(4,1)} %and_and_fusion) | copy-start | bytes 6291460
  151.2 5.2 %copy-start.15 = (f32[1024,2,128]{2,0,1:T(8,128)S(1)}, f32[1024,2,128]{2,0,1:T(8,128)}, u32[]{:S(2)}) copy-start(f32[1024,2,128]{2,0,1:T(8,128)} %copy.196) | copy-start | bytes 3145732
  161.3 5.7 %copy-start.5 = (f32[2,1024,2048]{2,1,0:T(8,128)}, f32[2,1024,2048]{2,1,0:T(8,128)S(1)}, u32[]{:S(2)}) copy-start(f32[2,1024,2048]{2,1,0:T(8,128)S(1)} %get-tuple-element.213) | copy-start | bytes 50331652
  161.4 5.7 %copy-start.22 = (bf16[16,2,128]{2,1,0:T(2,128)(2,1)S(1)}, bf16[16,2,128]{2,1,0:T(2,128)(2,1)}, u32[]{:S(2)}) copy-start(bf16[16,2,128]{2,1,0:T(2,128)(2,1)} %reshape_squeeze.7) | copy-start | bytes 24580
  182.1 10.5 %copy-start.17 = (bf16[256,1024]{1,0:T(8,128)(2,1)S(1)}, bf16[256,1024]{1,0:T(8,128)(2,1)}, u32[]{:S(2)}) copy-start(bf16[256,1024]{1,0:T(8,128)(2,1)} %param.19) | copy-start | bytes 1572868
  195.3 90.3 %copy-start.6 = (bf16[256,1024]{1,0:T(8,128)(2,1)S(1)}, bf16[256,1024]{1,0:T(8,128)(2,1)}, u32[]{:S(2)}) copy-start(bf16[256,1024]{1,0:T(8,128)(2,1)} %param.17) | copy-start | bytes 1572868
  195.3 91.8 %copy-start.23 = (f32[1,1024]{1,0:T(1,128)S(1)}, f32[1,1024]{1,0:T(1,128)}, u32[]{:S(2)}) copy-start(f32[1,1024]{1,0:T(1,128)} %get-tuple-element.206) | copy-start | bytes 12292
  195.3 139.4 %all-gather.12.cloned.1.call-start = ((), (), s32[]{:S(2)}) async-start(), calls=%async_computation.4 | async-start | bytes 2621440 | tf_op jit(solution)/shard_map/all_gather | solution.py:80
  288.1 131.2 %reduce-scatter.5.cloned.1.call-start = ((), (), s32[]{:S(2)}) async-start(), calls=%async_computation.5 | async-start | bytes 5242880 | tf_op jit(solution)/shard_map/reduce_scatter | solution.py:84
  334.7 5.2 %copy-start.31 = (bf16[704,1024]{1,0:T(8,128)(2,1)S(1)}, bf16[704,1024]{1,0:T(8,128)(2,1)}, u32[]{:S(2)}) copy-start(bf16[704,1024]{1,0:T(8,128)(2,1)} %param.21) | copy-start | bytes 4325380
  343.7 126.3 %all-gather.14.cloned.1.call-start = ((), (), s32[]{:S(2)}) async-start(), calls=%async_computation.6 | async-start | bytes 2621440 | tf_op jit(solution)/shard_map/all_gather | solution.py:80
  (18 other events, 45.7 us)
Sparse Core Ops, SparseCore 0:
  9.6 48.6 all-gather.9
  112.9 23.5 all-gather.17
  151.2 21.4 all-gather.15
  195.5 90.0 reduce-scatter.2
  288.2 46.4 all-gather.11
  343.9 75.4 reduce-scatter.4
  423.4 46.6 all-gather.13
